TPU v7x, 128 devices: a whole 4x4x4 slice. The times are simulated.
128 devices in a mesh: dp: 2 (over y_hi), pipe: 4 (over y_lo, core), chan: 16 (over x, z).
Axes of the slice: x: 4, y: 4 (y_hi: 2, y_lo: 2; y = y_hi * 2 + y_lo), z: 4, core: 2. Of those that a mesh axis runs over, the one named last changes fastest.
Arguments:
- latents: bfloat16 [2, 4, 640, 512], P('dp', None, 'chan'), may hold values from -6 to 6
- cotangent: bfloat16 [2, 4, 640, 512], P('dp', None, 'chan'), may hold values from -6 to 6
- order: int32 [2, 4], P('dp'), may hold values from 0 to 3, each once within a row
- tstep: int32 [2, 4], P('dp'), may hold values from 0 to 999
- emb_table: float32 [1000, 4, 640], P(None, None, 'chan'), may hold values from -5 to 5
- gn_gain: float32 [4, 640], P(None, 'chan'), may hold values from 0.1 to 1.9
- weights: bfloat16 [4, 27, 640, 640], P(None, None, 'chan'), may hold values from -0.0625 to 0.0625
Outputs:
- grad_weights: float32 [4, 27, 640, 640], P('pipe', None, 'chan')
Inputs may be any that keep to these rules, and one draw needn't show every extreme that they name: Each row of order names every micro-batch once.
All inputs are finite; a program needn't handle non-finite values.
Results may differ from a plain program's by a relative error of at most 0.015.
Values may be sent and summed in bfloat16 or wider, within the bound.
No kernel may reach another device: no remote copies, remote signals or barrier semaphores. Data moves between devices by JAX's collectives and lax.ppermute only.
A program may use at most 128 MiB of HBM per device.

v0:
```python
from functools import partial

import jax
import jax.numpy as jnp
from jax import lax
from jax.sharding import PartitionSpec as P

C = 640
GROUPS = 32
FR = 2
HT = 16
WD = 16


EPSILON = 1e-05


def passed_along(value, axis, steps):
    count = lax.axis_size(axis)
    first, last = (max(0, -steps), min(count, count - steps))
    return lax.ppermute(value, axis, [(source, source + steps) for source in range(first, last)])


def from_partner(value, axis, apart):
    mask = 2**apart
    pairs = [(source, source ^ mask) for source in range(lax.axis_size(axis))]
    return lax.ppermute(value, axis, pairs)


def pre_act(field, gain, offset):
    channels, places = field.shape
    grouped = field.reshape(channels // (C // GROUPS), -1)
    centred = grouped - jnp.mean(grouped, axis=1, keepdims=True)
    spread = jnp.mean(centred * centred, axis=1, keepdims=True)
    normed = (centred * lax.rsqrt(spread + EPSILON)).reshape(channels, places)
    return jax.nn.silu(normed * gain[:, None] + offset[:, None])


def tap_stack(field):
    places = field.shape[1]
    plane = HT * WD
    margin = plane + WD + 1
    padded = jnp.pad(field, ((0, 0), (margin, margin)))
    position = jnp.arange(places, dtype=jnp.int32)
    frame_at = position // plane
    line_at = position // WD % HT
    column_at = position % WD
    pieces = []
    for shift_f in (-1, 0, 1):
        for shift_h in (-1, 0, 1):
            for shift_w in (-1, 0, 1):
                offset = shift_f * plane + shift_h * WD + shift_w
                inside = (frame_at + shift_f >= 0) & (frame_at + shift_f < FR)
                inside = inside & (line_at + shift_h >= 0) & (line_at + shift_h < HT)
                inside = inside & (column_at + shift_w >= 0) & (column_at + shift_w < WD)
                moved = lax.slice_in_dim(padded, margin + offset, margin + offset + places, axis=1)
                pieces.append(jnp.where(inside[None, :], moved, jnp.zeros_like(moved)))
    return jnp.concatenate(pieces, axis=0)


def tap_adjoint(grads, channels, places):
    pull = jax.vjp(tap_stack, jnp.zeros((channels, places), jnp.float32))[1]
    return pull(grads)[0]


def partial_term(weight_rows, front):
    return lax.dot_general(
        weight_rows, front, (((0,), (0,)), ((), ())), preferred_element_type=jnp.float32
    )


def conv_sum(weight_rows, front):
    return lax.psum_scatter(
        partial_term(weight_rows, front).astype(jnp.bfloat16),
        "chan",
        scatter_dimension=0,
        tiled=True,
    ).astype(jnp.float32)


def fold_grads(grad_taps, grad_weight, piece, weight_rows, front):
    grad_taps = jnp.dot(weight_rows, piece, preferred_element_type=jnp.float32)
    previous = grad_weight
    update = lax.dot_general(
        front, piece, (((1,), (1,)), ((), ())), preferred_element_type=jnp.float32
    )
    grad_weight = previous + update
    return (grad_taps, grad_weight)


def grad_fold(grad, weight_rows, front, grad_weight):
    empty = jnp.zeros(front.shape, jnp.float32)
    return fold_grads(
        empty, grad_weight, lax.all_gather(grad, "chan", axis=0, tiled=True), weight_rows, front
    )


def per_device(latents, cotangent, order, tstep, emb_table, gn_gain, weights):
    pipe_count = lax.axis_size("pipe")
    section_rank = lax.axis_index("pipe")
    mirror_rank = pipe_count - 1 - section_rank
    channels = latents.shape[2]
    places = latents.shape[3]
    slot_count = latents.shape[1]
    half_slots = slot_count // 2
    width = weights.shape[3]
    order_row = order[0]
    timestep_row = tstep[0]
    slot_ids = jnp.arange(slot_count, dtype=jnp.int32)
    picked = jnp.sum(
        jnp.where(order_row[:, None] == slot_ids[None, :], timestep_row[None, :], 0), axis=1
    )
    step_ids = jnp.arange(emb_table.shape[0], dtype=jnp.int32)
    one_hot = (picked[:, None] == step_ids[None, :]).astype(jnp.float32)
    entries_all = jnp.take(latents[0], order_row, axis=0)
    sections = (section_rank, mirror_rank)
    rows_list = []
    gains = []
    offsets_list = []
    inputs = []
    cotans = []
    for direction in range(2):
        section = sections[direction]
        rows_list.append(
            lax.dynamic_index_in_dim(weights, section, 0, keepdims=False).reshape(
                27 * channels, width
            )
        )
        gains.append(lax.dynamic_index_in_dim(gn_gain, section, 0, keepdims=False))
        table = lax.dynamic_index_in_dim(emb_table, section, 1, keepdims=False)
        hot_rows = one_hot[direction * half_slots : (direction + 1) * half_slots]
        offsets_list.append(jnp.dot(hot_rows, table, precision=lax.Precision.HIGHEST))
        inputs.append(entries_all[direction * half_slots : (direction + 1) * half_slots])
        cotans.append(cotangent[0, direction * half_slots : (direction + 1) * half_slots])
    ticks = pipe_count + half_slots - 1
    zero_field = jnp.zeros((channels, places), jnp.bfloat16)
    received = [zero_field, zero_field]
    stores = [jnp.zeros((half_slots, channels, places), jnp.bfloat16) for direction in range(2)]
    for tick_index in range(ticks):
        fronts = []
        entries_now = []
        for direction in range(2):
            section = sections[direction]
            micro = tick_index - section
            is_live = (micro >= 0) & (micro < half_slots)
            clipped = jnp.clip(micro, 0, half_slots - 1)
            fresh = lax.dynamic_index_in_dim(inputs[direction], clipped, 0, keepdims=False)
            entry = jnp.where(section == 0, fresh, received[direction])
            kept = lax.dynamic_index_in_dim(stores[direction], clipped, 0, keepdims=False)
            stores[direction] = lax.dynamic_update_index_in_dim(
                stores[direction], jnp.where(is_live, entry, kept), clipped, 0
            )
            offset = lax.dynamic_index_in_dim(offsets_list[direction], clipped, 0, keepdims=False)
            active = pre_act(entry.astype(jnp.float32), gains[direction], offset).astype(
                jnp.bfloat16
            )
            fronts.append(tap_stack(active))
            entries_now.append(entry)
        sums = [conv_sum(rows_list[direction], fronts[direction]) for direction in range(2)]
        results = [
            (entries_now[direction].astype(jnp.float32) + sums[direction]).astype(jnp.bfloat16)
            for direction in range(2)
        ]
        if tick_index + 1 < ticks:
            received = [passed_along(results[0], "pipe", 1), passed_along(results[1], "pipe", -1)]
    grads_in = [zero_field, zero_field]
    accums = [jnp.zeros((27 * channels, width), jnp.float32) for direction in range(2)]
    for tick_index in range(ticks):
        live_grads = []
        fronts = []
        pullers = []
        for direction in range(2):
            section = sections[direction]
            micro = tick_index - (pipe_count - 1 - section)
            is_live = (micro >= 0) & (micro < half_slots)
            clipped = jnp.clip(micro, 0, half_slots - 1)
            fresh = lax.dynamic_index_in_dim(cotans[direction], clipped, 0, keepdims=False)
            incoming = jnp.where(section == pipe_count - 1, fresh, grads_in[direction])
            live_grads.append(jnp.where(is_live, incoming, zero_field))
            entry = lax.dynamic_index_in_dim(stores[direction], clipped, 0, keepdims=False)
            offset = lax.dynamic_index_in_dim(offsets_list[direction], clipped, 0, keepdims=False)
            active, pull = jax.vjp(
                partial(pre_act, gain=gains[direction], offset=offset), entry.astype(jnp.float32)
            )
            fronts.append(tap_stack(active.astype(jnp.bfloat16)))
            pullers.append(pull)
        folded = [
            grad_fold(
                live_grads[direction], rows_list[direction], fronts[direction], accums[direction]
            )
            for direction in range(2)
        ]
        sends = []
        for direction in range(2):
            grad_taps, accums[direction] = folded[direction]
            back = pullers[direction](tap_adjoint(grad_taps, channels, places))[0]
            sends.append((live_grads[direction].astype(jnp.float32) + back).astype(jnp.bfloat16))
        if tick_index + 1 < ticks:
            grads_in = [passed_along(sends[0], "pipe", -1), passed_along(sends[1], "pipe", 1)]
    mirrored = accums[1]
    for bit_index in range(pipe_count.bit_length() - 1):
        mirrored = from_partner(mirrored.astype(jnp.bfloat16), "pipe", bit_index).astype(
            mirrored.dtype
        )
    combined = accums[0] + mirrored
    total = lax.psum(combined.astype(jnp.bfloat16), "dp").astype(jnp.float32)
    return total.reshape(1, 27, channels, width)


def solution(mesh):
    return jax.shard_map(
        per_device,
        mesh=mesh,
        in_specs=(
            P("dp", None, "chan", None),
            P("dp", None, "chan", None),
            P("dp", None),
            P("dp", None),
            P(None, None, "chan"),
            P(None, "chan"),
            P(None, None, "chan", None),
        ),
        out_specs=P("pipe", None, "chan", None),
        check_vma=False,
    )
```

profile of v0, /device:TPU:1, one launch (start us, length us, event | category | flops | bytes accessed | tf_op | source)
XLA Modules:
  0.0 1002.4 jit_solution(15503735003179676090)
XLA Ops:
  20.3 75.4 %reduce-scatter.33.cloned.1.call-done = bf16[40,512]{1,0:T(8,128)(2,1)} async-done(((bf16[640,512]{1,0:T(8,128)(2,1)}), bf16[40,512]{1,0:T(8,128)(2,1)}) %reduce-scatter.33.cloned.1.call-update) | async-done | bytes 40976
  110.1 69.6 %reduce-scatter.35.cloned.1.call-done = bf16[40,512]{1,0:T(8,128)(2,1)} async-done(((bf16[640,512]{1,0:T(8,128)(2,1)}), bf16[40,512]{1,0:T(8,128)(2,1)}) %reduce-scatter.35.cloned.1.call-update) | async-done | bytes 40976
  193.5 18.8 %all-gather.1 = bf16[1,1,640,512]{3,2,1,0:T(8,128)(2,1)S(1)} all-gather(bf16[1,1,40,512]{3,2,1,0:T(8,128)(2,1)S(1)} %select_select_fusion), channel_id=3, replica_groups=mesh['dp'=2,'pipe'=4,'chan'=16] {'chan'}, dimensions={2}, use_global_device_ids=true | all-gather | bytes 696320 | tf_op jit(solution)/shard_map/all_gather | solution.py:94
  216.7 46.9 %reduce-scatter.37.cloned.1.call-done = bf16[40,512]{1,0:T(8,128)(2,1)} async-done(((bf16[640,512]{1,0:T(8,128)(2,1)}), bf16[40,512]{1,0:T(8,128)(2,1)}) %reduce-scatter.37.cloned.1.call-update) | async-done | bytes 40976
  278.4 19.3 %all-gather = bf16[1,1,640,512]{3,2,1,0:T(8,128)(2,1)S(1)} all-gather(bf16[1,1,40,512]{3,2,1,0:T(8,128)(2,1)S(1)} %select_select_fusion.1), channel_id=2, replica_groups=mesh['dp'=2,'pipe'=4,'chan'=16] {'chan'}, dimensions={2}, use_global_device_ids=true | all-gather | bytes 696320 | tf_op jit(solution)/shard_map/all_gather | solution.py:94
  302.7 46.2 %reduce-scatter.39.cloned.1.call-done = bf16[40,512]{1,0:T(8,128)(2,1)} async-done(((bf16[640,512]{1,0:T(8,128)(2,1)}), bf16[40,512]{1,0:T(8,128)(2,1)}) %reduce-scatter.39.cloned.1.call-update) | async-done | bytes 40976
  353.9 71.0 %reduce-scatter.25.cloned.1.call-done = bf16[40,512]{1,0:T(8,128)(2,1)} async-done(((bf16[640,512]{1,0:T(8,128)(2,1)}), bf16[40,512]{1,0:T(8,128)(2,1)}) %reduce-scatter.25.cloned.1.call-update) | async-done | bytes 40976
  425.7 5.3 collective-permute-start
  440.3 18.3 %all_gather.36 = bf16[640,512]{1,0:T(8,128)(2,1)S(1)} all-gather(bf16[40,512]{1,0:T(8,128)(2,1)S(1)} %fusion.768), channel_id=1, replica_groups=mesh['dp'=2,'pipe'=4,'chan'=16] {'chan'}, dimensions={0}, use_global_device_ids=true | all-gather | bytes 696320 | tf_op jit(solution)/shard_map/all_gather | solution.py:94
  464.9 8.1 collective-permute-start.13
  474.4 17.8 %all_gather.37 = bf16[640,512]{1,0:T(8,128)(2,1)S(1)} all-gather(bf16[40,512]{1,0:T(8,128)(2,1)S(1)} %fusion.767), channel_id=1, replica_groups=mesh['dp'=2,'pipe'=4,'chan'=16] {'chan'}, dimensions={0}, use_global_device_ids=true | all-gather | bytes 696320 | tf_op jit(solution)/shard_map/all_gather | solution.py:94
  497.3 8.1 collective-permute-start.14
  508.1 19.1 %all_gather.38 = bf16[640,512]{1,0:T(8,128)(2,1)S(1)} all-gather(bf16[40,512]{1,0:T(8,128)(2,1)S(1)} %fusion.766), channel_id=1, replica_groups=mesh['dp'=2,'pipe'=4,'chan'=16] {'chan'}, dimensions={0}, use_global_device_ids=true | all-gather | bytes 696320 | tf_op jit(solution)/shard_map/all_gather | solution.py:94
  546.9 7.1 collective-permute-start.15
  554.0 62.5 %reduce-scatter.27.cloned.1.call-done = bf16[40,512]{1,0:T(8,128)(2,1)} async-done(((bf16[640,512]{1,0:T(8,128)(2,1)}), bf16[40,512]{1,0:T(8,128)(2,1)}) %reduce-scatter.27.cloned.1.call-update) | async-done | bytes 40976
  637.6 19.7 %all_gather.39 = bf16[640,512]{1,0:T(8,128)(2,1)S(1)} all-gather(bf16[40,512]{1,0:T(8,128)(2,1)S(1)} %fusion.765), channel_id=1, replica_groups=mesh['dp'=2,'pipe'=4,'chan'=16] {'chan'}, dimensions={0}, use_global_device_ids=true | all-gather | bytes 696320 | tf_op jit(solution)/shard_map/all_gather | solution.py:94
  659.9 41.6 %reduce-scatter.29.cloned.1.call-done = bf16[40,512]{1,0:T(8,128)(2,1)} async-done(((bf16[640,512]{1,0:T(8,128)(2,1)}), bf16[40,512]{1,0:T(8,128)(2,1)}) %reduce-scatter.29.cloned.1.call-update) | async-done | bytes 40976
  702.3 5.7 collective-permute-start.2
  729.0 68.9 %reduce-scatter.31.cloned.1.call-done = bf16[40,512]{1,0:T(8,128)(2,1)} async-done(((bf16[640,512]{1,0:T(8,128)(2,1)}), bf16[40,512]{1,0:T(8,128)(2,1)}) %reduce-scatter.31.cloned.1.call-update) | async-done | bytes 40976
  815.4 18.4 %all_gather.31 = bf16[640,512]{1,0:T(8,128)(2,1)S(1)} all-gather(bf16[40,512]{1,0:T(8,128)(2,1)S(1)} %fusion.772), channel_id=1, replica_groups=mesh['dp'=2,'pipe'=4,'chan'=16] {'chan'}, dimensions={0}, use_global_device_ids=true | all-gather | bytes 696320 | tf_op jit(solution)/shard_map/all_gather | solution.py:94
  847.1 17.6 %all_gather.32 = bf16[640,512]{1,0:T(8,128)(2,1)S(1)} all-gather(bf16[40,512]{1,0:T(8,128)(2,1)S(1)} %fusion.771), channel_id=1, replica_groups=mesh['dp'=2,'pipe'=4,'chan'=16] {'chan'}, dimensions={0}, use_global_device_ids=true | all-gather | bytes 696320 | tf_op jit(solution)/shard_map/all_gather | solution.py:94
  876.0 19.1 %all_gather.33 = bf16[640,512]{1,0:T(8,128)(2,1)S(1)} all-gather(bf16[40,512]{1,0:T(8,128)(2,1)S(1)} %fusion.770), channel_id=1, replica_groups=mesh['dp'=2,'pipe'=4,'chan'=16] {'chan'}, dimensions={0}, use_global_device_ids=true | all-gather | bytes 696320 | tf_op jit(solution)/shard_map/all_gather | solution.py:94
  910.1 17.5 %all_gather.34 = bf16[640,512]{1,0:T(8,128)(2,1)S(1)} all-gather(bf16[40,512]{1,0:T(8,128)(2,1)S(1)} %fusion.769), channel_id=1, replica_groups=mesh['dp'=2,'pipe'=4,'chan'=16] {'chan'}, dimensions={0}, use_global_device_ids=true | all-gather | bytes 696320 | tf_op jit(solution)/shard_map/all_gather | solution.py:94
  932.7 59.9 %all-reduce.244.cloned.1.call-done = bf16[1,27,40,640]{3,2,1,0:T(8,128)(2,1)} async-done(((bf16[1,27,40,640]{3,2,1,0:T(8,128)(2,1)}), bf16[1,27,40,640]{3,2,1,0:T(8,128)(2,1)}) %all-reduce.244.cloned.1.call-update) | async-done | bytes 1382416 | tf_op jit(solution)/shard_map/psum | solution.py:206
  (1170 shorter events, 222.2 us)
Async XLA Ops:
  6.5 89.3 %reduce-scatter.33.cloned.1.call-start = ((), (), s32[]{:S(2)}) async-start(), calls=%async_computation.13 | async-start | bytes 696320
  20.3 159.4 %reduce-scatter.35.cloned.1.call-start = ((), (), s32[]{:S(2)}) async-start(), calls=%async_computation.14 | async-start | bytes 696320
  96.6 7.0 collective-permute-start.8
  108.9 154.7 %reduce-scatter.37.cloned.1.call-start = ((), (), s32[]{:S(2)}) async-start(), calls=%async_computation.15 | async-start | bytes 696320
  180.4 7.1 collective-permute-start.9
  192.8 156.0 %reduce-scatter.39.cloned.1.call-start = ((), (), s32[]{:S(2)}) async-start(), calls=%async_computation.16 | async-start | bytes 696320
  264.4 7.0 collective-permute-start.10
  278.1 146.8 %reduce-scatter.25.cloned.1.call-start = ((), (), s32[]{:S(2)}) async-start(), calls=%async_computation.9 | async-start | bytes 696320
  302.4 314.0 %reduce-scatter.27.cloned.1.call-start = ((), (), s32[]{:S(2)}) async-start(), calls=%async_computation.10 | async-start | bytes 696320
  349.6 81.4 %collective-permute-start.11 = (bf16[40,512]{1,0:T(8,128)(2,1)S(1)}, bf16[40,512]{1,0:T(8,128)(2,1)S(1)}, u32[]{:S(2)}, u32[]{:S(2)}) collective-permute-start(bf16[40,512]{1,0:T(8,128)(2,1)S(1)} %fusion.126), channel_id=1, source_target_pairs={{16,0},{32,16},{48,32},{17,1},{33,17},{49,33},{18,2},{34,18},{50,3... | collective-permute-start | bytes 122888 | tf_op jit(solution)/shard_map/ppermute | solution.py:21
  425.7 12.4 %collective-permute-start = (bf16[40,512]{1,0:T(8,128)(2,1)S(1)}, bf16[40,512]{1,0:T(8,128)(2,1)S(1)}, u32[]{:S(2)}, u32[]{:S(2)}) collective-permute-start(bf16[40,512]{1,0:T(8,128)(2,1)S(1)} %fusion.108), channel_id=1, source_target_pairs={{0,16},{16,32},{32,48},{1,17},{17,33},{33,49},{2,18},{18,34},{34,5... | collective-permute-start | bytes 122888 | tf_op jit(solution)/shard_map/ppermute | solution.py:21
  464.9 9.6 collective-permute-start.13
  497.3 10.8 %collective-permute-start.14 = (bf16[40,512]{1,0:T(8,128)(2,1)S(1)}, bf16[40,512]{1,0:T(8,128)(2,1)S(1)}, u32[]{:S(2)}, u32[]{:S(2)}) collective-permute-start(bf16[40,512]{1,0:T(8,128)(2,1)S(1)} %add_convert_fusion.2), channel_id=1, source_target_pairs={{0,16},{16,32},{32,48},{1,17},{17,33},{33,49},{2,18},{18,34},{34,5... | collective-permute-start | bytes 122888 | tf_op jit(solution)/shard_map/ppermute | solution.py:21
  542.3 159.2 %reduce-scatter.29.cloned.1.call-start = ((), (), s32[]{:S(2)}) async-start(), calls=%async_computation.11 | async-start | bytes 696320
  546.9 89.9 %collective-permute-start.15 = (bf16[40,512]{1,0:T(8,128)(2,1)}, bf16[40,512]{1,0:T(8,128)(2,1)}, u32[]{:S(2)}, u32[]{:S(2)}) collective-permute-start(bf16[40,512]{1,0:T(8,128)(2,1)} %add_convert_fusion.1), channel_id=1, source_target_pairs={{0,16},{16,32},{32,48},{1,17},{17,33},{33,49},{2,18},{18,34},{34,5... | collective-permute-start | bytes 122888 | tf_op jit(solution)/shard_map/ppermute | solution.py:21
  617.2 8.0 collective-permute-start.1
  630.7 167.2 %reduce-scatter.31.cloned.1.call-start = ((), (), s32[]{:S(2)}) async-start(), calls=%async_computation.12 | async-start | bytes 696320
  702.3 11.2 %collective-permute-start.2 = (bf16[40,512]{1,0:T(8,128)(2,1)S(1)}, bf16[40,512]{1,0:T(8,128)(2,1)S(1)}, u32[]{:S(2)}, u32[]{:S(2)}) collective-permute-start(bf16[40,512]{1,0:T(8,128)(2,1)S(1)} %fusion.110), channel_id=1, source_target_pairs={{0,16},{16,32},{32,48},{1,17},{17,33},{33,49},{2,18},{18,34},{34,5... | collective-permute-start | bytes 122888 | tf_op jit(solution)/shard_map/ppermute | solution.py:21
  713.4 15.4 %collective-permute-start.16 = (bf16[1080,640]{1,0:T(8,128)(2,1)}, bf16[1080,640]{1,0:T(8,128)(2,1)}, u32[]{:S(2)}, u32[]{:S(2)}) collective-permute-start(bf16[1080,640]{1,0:T(8,128)(2,1)} %fusion.4), channel_id=1, source_target_pairs={{0,16},{16,0},{32,48},{48,32},{1,17},{17,1},{33,49},{49,33},{2,18}... | collective-permute-start | bytes 4147208 | tf_op jit(solution)/shard_map/ppermute | solution.py:27
  726.8 265.8 %all-reduce.244.cloned.1.call-start = ((), (), s32[]{:S(2)}) async-start(), calls=%async_computation.8 | async-start | bytes 2764800 | tf_op jit(solution)/shard_map/psum | solution.py:206
  728.8 200.0 %collective-permute-start.17 = (bf16[1080,640]{1,0:T(8,128)(2,1)}, bf16[1080,640]{1,0:T(8,128)(2,1)}, u32[]{:S(2)}, u32[]{:S(2)}) collective-permute-start(bf16[1080,640]{1,0:T(8,128)(2,1)} %collective-permute-done.16), channel_id=1, source_target_pairs={{0,32},{16,48},{32,0},{48,16},{1,33},{17,49},{33,1},{49,17},{2,34}... | collective-permute-start | bytes 4147208 | tf_op jit(solution)/shard_map/ppermute | solution.py:27
  838.5 8.6 collective-permute-start.5
  868.1 8.0 collective-permute-start.6
  899.8 10.3 %collective-permute-start.7 = (bf16[40,512]{1,0:T(8,128)(2,1)S(1)}, bf16[40,512]{1,0:T(8,128)(2,1)S(1)}, u32[]{:S(2)}, u32[]{:S(2)}) collective-permute-start(bf16[40,512]{1,0:T(8,128)(2,1)S(1)} %add_convert_fusion.4), channel_id=1, source_target_pairs={{16,0},{32,16},{48,32},{17,1},{33,17},{49,33},{18,2},{34,18},{50,3... | collective-permute-start | bytes 122888 | tf_op jit(solution)/shard_map/ppermute | solution.py:21
  (237 other events, 10535.0 us)
Sparse Core Ops, SparseCore 0:
  20.4 75.3 reduce-scatter.32
  109.0 70.6 reduce-scatter.34
  192.9 70.5 reduce-scatter.36
  278.3 70.5 reduce-scatter.38
  351.8 73.0 reduce-scatter.24
  542.4 73.9 reduce-scatter.26
  630.8 70.6 reduce-scatter.28
  726.9 70.9 reduce-scatter.30
  932.8 59.7 all-reduce.243
where the time goes:
time: 1010 us; the launch traced here: 1000 us
  waiting for transfers between devices  563 us (56%)
  blocking collectives  186 us (18%)
  starting transfers between devices  77.6 us (8%)
  other arithmetic  71 us (7%)
  matrix products  54.5 us (5%)
  local copies, waits for them, and re-layouts  32.5 us (3%)
  between operations  18.2 us (2%)
    unnamed x17, waiting for transfers between devices  482 us
    all_gather x10, blocking collectives, grad_fold(): lax.all_gather(grad, 'chan', axis=0, tiled=True)  186 us
    ppermute x16, starting transfers between devices, passed_along(): lax.ppermute(value, axis, [(source, source + steps) for source in range(f...  77 us
    psum x1, waiting for transfers between devices, per_device(): total = lax.psum(combined.astype(jnp.bfloat16), 'dp').astype(jnp.float32)  59.9 us
    unnamed x208, other arithmetic  25.2 us
    dot_general x10, matrix products, fold_grads(): lax.dot_general(front, piece, (((1,), (1,)), ((), ())), preferred_element...  23.4 us
    ppermute x16, waiting for transfers between devices, passed_along(): lax.ppermute(value, axis, [(source, source + steps) for source in range(f...  20.6 us
  transfers between devices with their start and end apart: 27, of which 16 were waited for; matrix products, arithmetic and copies ran while one was open for 9% of the time, Pallas kernels for 0%

commit v1 on v0

--- a/solution.py
+++ b/solution.py
@@ -69,13 +69,27 @@
     )
 
 
-def conv_sum(weight_rows, front):
-    return lax.psum_scatter(
-        partial_term(weight_rows, front).astype(jnp.bfloat16),
-        "chan",
-        scatter_dimension=0,
-        tiled=True,
-    ).astype(jnp.float32)
+def conv_sums(rows_pair, fronts_pair):
+    count = lax.axis_size("chan")
+    parts = jnp.stack(
+        [
+            partial_term(rows, front).astype(jnp.bfloat16)
+            for rows, front in zip(rows_pair, fronts_pair)
+        ]
+    )
+    parts = parts.reshape(parts.shape[0], count, parts.shape[1] // count, parts.shape[2])
+    got = lax.all_to_all(parts, "chan", 1, 1, tiled=False)
+    sums = jnp.sum(got.astype(jnp.float32), axis=1)
+    return [sums[direction] for direction in range(sums.shape[0])]
+
+
+def gather_pair(grads_pair):
+    count = lax.axis_size("chan")
+    stacked = jnp.stack(grads_pair)
+    spread = jnp.broadcast_to(stacked[:, None], (stacked.shape[0], count) + stacked.shape[1:])
+    got = lax.all_to_all(spread, "chan", 1, 1, tiled=False)
+    got = got.reshape(got.shape[0], count * got.shape[2], got.shape[3])
+    return [got[direction] for direction in range(got.shape[0])]
 
 
 def fold_grads(grad_taps, grad_weight, piece, weight_rows, front):
@@ -88,11 +102,9 @@
     return (grad_taps, grad_weight)
 
 
-def grad_fold(grad, weight_rows, front, grad_weight):
+def grad_fold(full_grad, weight_rows, front, grad_weight):
     empty = jnp.zeros(front.shape, jnp.float32)
-    return fold_grads(
-        empty, grad_weight, lax.all_gather(grad, "chan", axis=0, tiled=True), weight_rows, front
-    )
+    return fold_grads(empty, grad_weight, full_grad, weight_rows, front)
 
 
 def per_device(latents, cotangent, order, tstep, emb_table, gn_gain, weights):
@@ -156,7 +168,7 @@
             )
             fronts.append(tap_stack(active))
             entries_now.append(entry)
-        sums = [conv_sum(rows_list[direction], fronts[direction]) for direction in range(2)]
+        sums = conv_sums(rows_list, fronts)
         results = [
             (entries_now[direction].astype(jnp.float32) + sums[direction]).astype(jnp.bfloat16)
             for direction in range(2)
@@ -184,9 +196,10 @@
             )
             fronts.append(tap_stack(active.astype(jnp.bfloat16)))
             pullers.append(pull)
+        full_grads = gather_pair(live_grads)
         folded = [
             grad_fold(
-                live_grads[direction], rows_list[direction], fronts[direction], accums[direction]
+                full_grads[direction], rows_list[direction], fronts[direction], accums[direction]
             )
             for direction in range(2)
         ]

time: 1010 us -> 494 us (0.49)
  waiting for transfers between devices: 563 us -> 215 us
  blocking collectives: 186 us -> 0 us
  matrix products: 54.5 us -> 30.6 us
  starting transfers between devices: 77.6 us -> 92.1 us
  local copies, waits for them, and re-layouts: 32.5 us -> 46.6 us
  other arithmetic: 71 us -> 81.2 us
    unnamed x17 -> x1, waiting for transfers between devices: 482 us -> 0.02 us
    all_gather x10 -> x0, blocking collectives: 186 us -> none  [grad_fold(): lax.all_gather(grad, 'chan', axis=0, tiled=True)]
    all_to_all x0 -> x9, waiting for transfers between devices: none -> 130 us  [the longest x5 69.1 us: gather_pair(): got = lax.all_to_all(spread, 'chan', 1, 1, tiled=False)]
    all_to_all x0 -> x9, starting transfers between devices: none -> 43.1 us  [the longest x4 22.8 us: conv_sums(): got = lax.all_to_all(parts, 'chan', 1, 1, tiled=False)]
    ppermute x16, starting transfers between devices: 77 us -> 48.4 us  [passed_along(): lax.ppermute(value, axis, [(source, source + steps) for source in range(f...]
    ppermute x2, waiting for transfers between devices: 0.01 us -> 28.1 us  [from_partner(): return lax.ppermute(value, axis, pairs)]
    ppermute x16, waiting for transfers between devices: 20.6 us -> 4.3 us  [passed_along(): lax.ppermute(value, axis, [(source, source + steps) for source in range(f...]
    dot_general x10, matrix products: 23.4 us -> 12.3 us  [fold_grads(): lax.dot_general(front, piece, (((1,), (1,)), ((), ())), preferred_element...]
  transfers between devices with their start and end apart: 27 -> 28, of which waited for: 16 -> 16; matrix products, arithmetic and copies ran while one was open for 9% -> 13% of each run, Pallas kernels for 0% -> 0%
where the time goes in v1:
time: 494 us; the launch traced here: 485 us
  waiting for transfers between devices  215 us (44%)
  starting transfers between devices  92.1 us (19%)
  other arithmetic  81.2 us (16%)
  local copies, waits for them, and re-layouts  46.6 us (9%)
  matrix products  30.6 us (6%)
  between operations  18.6 us (4%)
    all_to_all x5, waiting for transfers between devices, gather_pair(): got = lax.all_to_all(spread, 'chan', 1, 1, tiled=False)  69.1 us
    all_to_all x4, waiting for transfers between devices, conv_sums(): got = lax.all_to_all(parts, 'chan', 1, 1, tiled=False)  60.6 us
    psum x1, waiting for transfers between devices, per_device(): total = lax.psum(combined.astype(jnp.bfloat16), 'dp').astype(jnp.float32)  53.3 us
    ppermute x16, starting transfers between devices, passed_along(): lax.ppermute(value, axis, [(source, source + steps) for source in range(f...  48.4 us
    ppermute x2, waiting for transfers between devices, from_partner(): return lax.ppermute(value, axis, pairs)  28.1 us
    all_to_all x4, starting transfers between devices, conv_sums(): got = lax.all_to_all(parts, 'chan', 1, 1, tiled=False)  22.8 us
    all_to_all x5, starting transfers between devices, gather_pair(): got = lax.all_to_all(spread, 'chan', 1, 1, tiled=False)  20.3 us
    unnamed x502, local copies, waits for them, and re-layouts  17.1 us
  transfers between devices with their start and end apart: 28, of which 16 were waited for; matrix products, arithmetic and copies ran while one was open for 13% of the time, Pallas kernels for 0%

profile of v1, /device:TPU:1, one launch (start us, length us, event | category | flops | bytes accessed | tf_op | source)
XLA Modules:
  0.0 484.6 jit_solution(3819780631851408894)
XLA Ops:
  22.3 8.5 %all-to-all-start = ((bf16[2,16,40,512]{3,2,0,1:T(8,128)(2,1)}), bf16[2,16,40,512]{3,2,0,1:T(8,128)(2,1)S(1)}, u32[]{:S(2)}, u32[]{:S(2)}) async-start(bf16[2,16,40,512]{3,2,0,1:T(8,128)(2,1)} %pad_maximum_fusion), calls=%async_computation | async-start | bytes 2621440 | tf_op jit(solution)/shard_map/all_to_all | solution.py:81
  31.0 18.0 %all-to-all-done = bf16[2,16,40,512]{3,2,0,1:T(8,128)(2,1)S(1)} async-done(((bf16[2,16,40,512]{3,2,0,1:T(8,128)(2,1)}), bf16[2,16,40,512]{3,2,0,1:T(8,128)(2,1)S(1)}, u32[]{:S(2)}, u32[]{:S(2)}) %all-to-all-start) | async-done | bytes 1310752 | tf_op jit(solution)/shard_map/all_to_all | solution.py:81
  50.3 4.5 all-to-all-start.4
  55.0 4.6 collective-permute-start.1
  72.2 6.9 %all-to-all-start.1 = ((bf16[2,16,40,512]{3,2,0,1:T(8,128)(2,1)}), bf16[2,16,40,512]{3,2,0,1:T(8,128)(2,1)S(1)}, u32[]{:S(2)}, u32[]{:S(2)}) async-start(bf16[2,16,40,512]{3,2,0,1:T(8,128)(2,1)} %pad_maximum_fusion.1), calls=%async_computation.1 | async-start | bytes 2621440 | tf_op jit(solution)/shard_map/all_to_all | solution.py:81
  84.5 13.8 %all-to-all-done.1 = bf16[2,16,40,512]{3,2,0,1:T(8,128)(2,1)S(1)} async-done(((bf16[2,16,40,512]{3,2,0,1:T(8,128)(2,1)}), bf16[2,16,40,512]{3,2,0,1:T(8,128)(2,1)S(1)}, u32[]{:S(2)}, u32[]{:S(2)}) %all-to-all-start.1) | async-done | bytes 1310752 | tf_op jit(solution)/shard_map/all_to_all | solution.py:81
  98.5 4.5 collective-permute-start.3
  114.1 3.7 all-to-all-start.2
  125.9 11.2 %all-to-all-done.2 = bf16[2,16,40,512]{3,2,0,1:T(8,128)(2,1)S(1)} async-done(((bf16[2,16,40,512]{3,2,0,1:T(8,128)(2,1)}), bf16[2,16,40,512]{3,2,0,1:T(8,128)(2,1)S(1)}, u32[]{:S(2)}, u32[]{:S(2)}) %all-to-all-start.2) | async-done | bytes 1310752 | tf_op jit(solution)/shard_map/all_to_all | solution.py:81
  137.4 4.3 collective-permute-start.5
  152.9 3.7 all-to-all-start.3
  158.9 17.6 %all-to-all-done.3 = bf16[2,16,40,512]{3,2,0,1:T(8,128)(2,1)S(1)} async-done(((bf16[2,16,40,512]{3,2,0,1:T(8,128)(2,1)}), bf16[2,16,40,512]{3,2,0,1:T(8,128)(2,1)S(1)}, u32[]{:S(2)}, u32[]{:S(2)}) %all-to-all-start.3) | async-done | bytes 1310752 | tf_op jit(solution)/shard_map/all_to_all | solution.py:81
  200.8 3.7 all-to-all-start.5
  206.4 18.3 %all-to-all-done.5 = bf16[2,16,40,512]{3,2,0,1:T(8,128)(2,1)S(1)} async-done(((bf16[2,16,40,512]{3,2,0,1:T(8,128)(2,1)}), bf16[2,16,40,512]{3,2,0,1:T(8,128)(2,1)S(1)}, u32[]{:S(2)}, u32[]{:S(2)}) %all-to-all-start.5) | async-done | bytes 1310752 | tf_op jit(solution)/shard_map/all_to_all | solution.py:90
  244.8 3.6 collective-permute-start.11
  251.4 3.8 all-to-all-start.6
  257.0 18.3 %all-to-all-done.6 = bf16[2,16,40,512]{3,2,0,1:T(8,128)(2,1)S(1)} async-done(((bf16[2,16,40,512]{3,2,0,1:T(8,128)(2,1)}), bf16[2,16,40,512]{3,2,0,1:T(8,128)(2,1)S(1)}, u32[]{:S(2)}, u32[]{:S(2)}) %all-to-all-start.6) | async-done | bytes 1310752 | tf_op jit(solution)/shard_map/all_to_all | solution.py:90
  295.5 3.6 collective-permute-start.13
  301.5 3.9 all-to-all-start.7
  306.9 18.6 %all-to-all-done.7 = bf16[2,16,40,512]{3,2,0,1:T(8,128)(2,1)S(1)} async-done(((bf16[2,16,40,512]{3,2,0,1:T(8,128)(2,1)}), bf16[2,16,40,512]{3,2,0,1:T(8,128)(2,1)S(1)}, u32[]{:S(2)}, u32[]{:S(2)}) %all-to-all-start.7) | async-done | bytes 1310752 | tf_op jit(solution)/shard_map/all_to_all | solution.py:90
  357.3 4.4 all-to-all-start.8
  367.8 13.9 %all-to-all-done.8 = bf16[2,16,40,512]{3,2,0,1:T(8,128)(2,1)} async-done(((bf16[2,16,40,512]{3,2,0,1:T(8,128)(2,1)}), bf16[2,16,40,512]{3,2,0,1:T(8,128)(2,1)}, u32[]{:S(2)}, u32[]{:S(2)}) %all-to-all-start.8) | async-done | bytes 1310752 | tf_op jit(solution)/shard_map/all_to_all | solution.py:90
  393.2 26.3 %collective-permute-done.17 = bf16[1080,640]{1,0:T(8,128)(2,1)S(1)} collective-permute-done((bf16[1080,640]{1,0:T(8,128)(2,1)S(1)}, bf16[1080,640]{1,0:T(8,128)(2,1)S(1)}, u32[]{:S(2)}, u32[]{:S(2)}) %collective-permute-start.17) | collective-permute-done | bytes 1382432 | tf_op jit(solution)/shard_map/ppermute | solution.py:27
  420.9 53.3 %all-reduce.236.cloned.1.call-done = bf16[1,27,40,640]{3,2,1,0:T(8,128)(2,1)} async-done(((bf16[1,27,40,640]{3,2,1,0:T(8,128)(2,1)}), bf16[1,27,40,640]{3,2,1,0:T(8,128)(2,1)}) %all-reduce.236.cloned.1.call-update) | async-done | bytes 1382416 | tf_op jit(solution)/shard_map/psum | solution.py:219
  (1151 shorter events, 192.8 us)
Async XLA Ops:
  22.3 26.8 %all-to-all-start = ((bf16[2,16,40,512]{3,2,0,1:T(8,128)(2,1)}), bf16[2,16,40,512]{3,2,0,1:T(8,128)(2,1)S(1)}, u32[]{:S(2)}, u32[]{:S(2)}) async-start(bf16[2,16,40,512]{3,2,0,1:T(8,128)(2,1)} %pad_maximum_fusion), calls=%async_computation | async-start | bytes 2621440 | tf_op jit(solution)/shard_map/all_to_all | solution.py:81
  50.3 21.8 %all-to-all-start.4 = ((bf16[2,16,40,512]{3,2,0,1:T(8,128)(2,1)}), bf16[2,16,40,512]{3,2,0,1:T(8,128)(2,1)S(1)}, u32[]{:S(2)}, u32[]{:S(2)}) async-start(bf16[2,16,40,512]{3,2,0,1:T(8,128)(2,1)} %broadcast_in_dim.4741), calls=%async_computation.4 | async-start | bytes 2621440 | tf_op jit(solution)/shard_map/all_to_all | solution.py:90
  55.0 8.4 %collective-permute-start.1 = (bf16[40,512]{1,0:T(8,128)(2,1)S(1)}, bf16[40,512]{1,0:T(8,128)(2,1)S(1)}, u32[]{:S(2)}, u32[]{:S(2)}) collective-permute-start(bf16[40,512]{1,0:T(8,128)(2,1)S(1)} %get-tuple-element.289), channel_id=1, source_target_pairs={{16,0},{32,16},{48,32},{17,1},{33,17},{49,33},{18,2},{34,18},{50,3... | collective-permute-start | bytes 122888 | tf_op jit(solution)/shard_map/ppermute | solution.py:21
  72.2 26.1 %all-to-all-start.1 = ((bf16[2,16,40,512]{3,2,0,1:T(8,128)(2,1)}), bf16[2,16,40,512]{3,2,0,1:T(8,128)(2,1)S(1)}, u32[]{:S(2)}, u32[]{:S(2)}) async-start(bf16[2,16,40,512]{3,2,0,1:T(8,128)(2,1)} %pad_maximum_fusion.1), calls=%async_computation.1 | async-start | bytes 2621440 | tf_op jit(solution)/shard_map/all_to_all | solution.py:81
  98.5 6.9 %collective-permute-start.3 = (bf16[40,512]{1,0:T(8,128)(2,1)S(1)}, bf16[40,512]{1,0:T(8,128)(2,1)S(1)}, u32[]{:S(2)}, u32[]{:S(2)}) collective-permute-start(bf16[40,512]{1,0:T(8,128)(2,1)S(1)} %get-tuple-element.287), channel_id=1, source_target_pairs={{16,0},{32,16},{48,32},{17,1},{33,17},{49,33},{18,2},{34,18},{50,3... | collective-permute-start | bytes 122888 | tf_op jit(solution)/shard_map/ppermute | solution.py:21
  114.1 23.0 %all-to-all-start.2 = ((bf16[2,16,40,512]{3,2,0,1:T(8,128)(2,1)}), bf16[2,16,40,512]{3,2,0,1:T(8,128)(2,1)S(1)}, u32[]{:S(2)}, u32[]{:S(2)}) async-start(bf16[2,16,40,512]{3,2,0,1:T(8,128)(2,1)} %pad_maximum_fusion.2), calls=%async_computation.2 | async-start | bytes 2621440 | tf_op jit(solution)/shard_map/all_to_all | solution.py:81
  137.4 6.3 %collective-permute-start.5 = (bf16[40,512]{1,0:T(8,128)(2,1)S(1)}, bf16[40,512]{1,0:T(8,128)(2,1)S(1)}, u32[]{:S(2)}, u32[]{:S(2)}) collective-permute-start(bf16[40,512]{1,0:T(8,128)(2,1)S(1)} %get-tuple-element.285), channel_id=1, source_target_pairs={{16,0},{32,16},{48,32},{17,1},{33,17},{49,33},{18,2},{34,18},{50,3... | collective-permute-start | bytes 122888 | tf_op jit(solution)/shard_map/ppermute | solution.py:21
  152.9 23.5 %all-to-all-start.3 = ((bf16[2,16,40,512]{3,2,0,1:T(8,128)(2,1)}), bf16[2,16,40,512]{3,2,0,1:T(8,128)(2,1)S(1)}, u32[]{:S(2)}, u32[]{:S(2)}) async-start(bf16[2,16,40,512]{3,2,0,1:T(8,128)(2,1)} %pad_maximum_fusion.3), calls=%async_computation.3 | async-start | bytes 2621440 | tf_op jit(solution)/shard_map/all_to_all | solution.py:81
  176.7 5.2 %collective-permute-start.6 = (bf16[40,512]{1,0:T(8,128)(2,1)S(1)}, bf16[40,512]{1,0:T(8,128)(2,1)S(1)}, u32[]{:S(2)}, u32[]{:S(2)}) collective-permute-start(bf16[40,512]{1,0:T(8,128)(2,1)S(1)} %get-tuple-element.282), channel_id=1, source_target_pairs={{0,16},{16,32},{32,48},{1,17},{17,33},{33,49},{2,18},{18,34},{34,5... | collective-permute-start | bytes 122888 | tf_op jit(solution)/shard_map/ppermute | solution.py:21
  179.0 10.8 %collective-permute-start.8 = (bf16[40,512]{1,0:T(8,128)(2,1)S(1)}, bf16[40,512]{1,0:T(8,128)(2,1)S(1)}, u32[]{:S(2)}, u32[]{:S(2)}) collective-permute-start(bf16[40,512]{1,0:T(8,128)(2,1)S(1)} %get-tuple-element.281), channel_id=1, source_target_pairs={{16,0},{32,16},{48,32},{17,1},{33,17},{49,33},{18,2},{34,18},{50,3... | collective-permute-start | bytes 122888 | tf_op jit(solution)/shard_map/ppermute | solution.py:21
  187.7 10.8 %collective-permute-start.7 = (bf16[40,512]{1,0:T(8,128)(2,1)S(1)}, bf16[40,512]{1,0:T(8,128)(2,1)S(1)}, u32[]{:S(2)}, u32[]{:S(2)}) collective-permute-start(bf16[40,512]{1,0:T(8,128)(2,1)S(1)} %fusion.284), channel_id=1, source_target_pairs={{16,0},{32,16},{48,32},{17,1},{33,17},{49,33},{18,2},{34,18},{50,3... | collective-permute-start | bytes 122888 | tf_op jit(solution)/shard_map/ppermute | solution.py:21
  194.9 4.7 collective-permute-start.9
  200.8 23.8 %all-to-all-start.5 = ((bf16[2,16,40,512]{3,2,0,1:T(8,128)(2,1)}), bf16[2,16,40,512]{3,2,0,1:T(8,128)(2,1)S(1)}, u32[]{:S(2)}, u32[]{:S(2)}) async-start(bf16[2,16,40,512]{3,2,0,1:T(8,128)(2,1)} %broadcast_in_dim.4759), calls=%async_computation.5 | async-start | bytes 2621440 | tf_op jit(solution)/shard_map/all_to_all | solution.py:90
  237.1 11.3 %collective-permute-start.10 = (bf16[40,512]{1,0:T(8,128)(2,1)}, bf16[40,512]{1,0:T(8,128)(2,1)S(1)}, u32[]{:S(2)}, u32[]{:S(2)}) collective-permute-start(bf16[40,512]{1,0:T(8,128)(2,1)} %add_convert_fusion.6), channel_id=1, source_target_pairs={{16,0},{32,16},{48,32},{17,1},{33,17},{49,33},{18,2},{34,18},{50,3... | collective-permute-start | bytes 122888 | tf_op jit(solution)/shard_map/ppermute | solution.py:21
  244.8 4.7 collective-permute-start.11
  251.4 23.9 %all-to-all-start.6 = ((bf16[2,16,40,512]{3,2,0,1:T(8,128)(2,1)}), bf16[2,16,40,512]{3,2,0,1:T(8,128)(2,1)S(1)}, u32[]{:S(2)}, u32[]{:S(2)}) async-start(bf16[2,16,40,512]{3,2,0,1:T(8,128)(2,1)} %broadcast_in_dim.4772), calls=%async_computation.6 | async-start | bytes 2621440 | tf_op jit(solution)/shard_map/all_to_all | solution.py:90
  287.8 11.3 %collective-permute-start.12 = (bf16[40,512]{1,0:T(8,128)(2,1)}, bf16[40,512]{1,0:T(8,128)(2,1)S(1)}, u32[]{:S(2)}, u32[]{:S(2)}) collective-permute-start(bf16[40,512]{1,0:T(8,128)(2,1)} %add_convert_fusion.4), channel_id=1, source_target_pairs={{16,0},{32,16},{48,32},{17,1},{33,17},{49,33},{18,2},{34,18},{50,3... | collective-permute-start | bytes 122888 | tf_op jit(solution)/shard_map/ppermute | solution.py:21
  295.5 4.7 collective-permute-start.13
  301.5 24.0 %all-to-all-start.7 = ((bf16[2,16,40,512]{3,2,0,1:T(8,128)(2,1)}), bf16[2,16,40,512]{3,2,0,1:T(8,128)(2,1)S(1)}, u32[]{:S(2)}, u32[]{:S(2)}) async-start(bf16[2,16,40,512]{3,2,0,1:T(8,128)(2,1)} %broadcast_in_dim.4785), calls=%async_computation.7 | async-start | bytes 2621440 | tf_op jit(solution)/shard_map/all_to_all | solution.py:90
  347.6 7.3 %collective-permute-start.14 = (bf16[40,512]{1,0:T(8,128)(2,1)S(1)}, bf16[40,512]{1,0:T(8,128)(2,1)S(1)}, u32[]{:S(2)}, u32[]{:S(2)}) collective-permute-start(bf16[40,512]{1,0:T(8,128)(2,1)S(1)} %add_convert_fusion.2), channel_id=1, source_target_pairs={{16,0},{32,16},{48,32},{17,1},{33,17},{49,33},{18,2},{34,18},{50,3... | collective-permute-start | bytes 122888 | tf_op jit(solution)/shard_map/ppermute | solution.py:21
  351.3 4.7 collective-permute-start.15
  357.3 24.5 %all-to-all-start.8 = ((bf16[2,16,40,512]{3,2,0,1:T(8,128)(2,1)}), bf16[2,16,40,512]{3,2,0,1:T(8,128)(2,1)}, u32[]{:S(2)}, u32[]{:S(2)}) async-start(bf16[2,16,40,512]{3,2,0,1:T(8,128)(2,1)} %broadcast_in_dim.4798), calls=%async_computation.8 | async-start | bytes 2621440 | tf_op jit(solution)/shard_map/all_to_all | solution.py:90
  361.7 112.6 %all-reduce.236.cloned.1.call-start = ((), (), s32[]{:S(2)}) async-start(), calls=%async_computation.9 | async-start | bytes 2764800 | tf_op jit(solution)/shard_map/psum | solution.py:219
  387.7 31.7 %collective-permute-start.17 = (bf16[1080,640]{1,0:T(8,128)(2,1)S(1)}, bf16[1080,640]{1,0:T(8,128)(2,1)S(1)}, u32[]{:S(2)}, u32[]{:S(2)}) collective-permute-start(bf16[1080,640]{1,0:T(8,128)(2,1)S(1)} %collective-permute-done.16), channel_id=1, source_target_pairs={{0,32},{16,48},{32,0},{48,16},{1,33},{17,49},{33,1},{49,17},{2,34}... | collective-permute-start | bytes 4147208 | tf_op jit(solution)/shard_map/ppermute | solution.py:27
  (255 other events, 4044.8 us)
Sparse Core Ops, SparseCore 0:
  421.0 53.1 all-reduce.235
